TPU v7x, 256 devices: a whole 4x4x8 slice. The times are simulated.
256 devices in a mesh: dp: 16 (over z_lo, x), tensor: 16 (over z_hi, y, core).
Axes of the slice: x: 4, y: 4, z: 8 (z_hi: 2, z_lo: 4; z = z_hi * 4 + z_lo), core: 2. Of those that a mesh axis runs over, the one named last changes fastest.
Arguments:
- cotangent: bfloat16 [8192, 4096], P(('dp', 'tensor')), may hold values from -6 to 6
- gate: bfloat16 [8192, 14336], P('dp', 'tensor'), may hold values from -8 to 8
- up: bfloat16 [8192, 14336], P('dp', 'tensor'), may hold values from -6 to 6
- w_down: bfloat16 [4, 14336, 4096], P(None, 'tensor', 'dp'), may hold values from -0.03125 to 0.03125
- language: int32 [16], replicated, may hold values from 0 to 3
Outputs:
- d_gate: bfloat16 [8192, 14336], P('dp', 'tensor')
- d_up: bfloat16 [8192, 14336], P('dp', 'tensor')
- d_weight: float32 [4, 14336, 4096], P(None, 'tensor', 'dp')
All inputs are finite; a program needn't handle non-finite values.
Results may differ from a plain program's by a relative error of at most 0.0029.
Values may be sent and summed in bfloat16 or wider, within the bound.
No kernel may reach another device: no remote copies, remote signals or barrier semaphores. Data moves between devices by JAX's collectives and lax.ppermute only.
A program may use at most 128 MiB of HBM per device.

v0:
```python
import jax
import jax.numpy as jnp
from jax import lax
from jax.sharding import PartitionSpec as P


def shards(cotangent, gate, up, w_down, language):
    groups = lax.axis_size("dp")
    variants = w_down.shape[0]
    ff_dev = w_down.shape[1]
    feat_dev = w_down.shape[2]
    out_rows = lax.all_gather(cotangent, "tensor", axis=0, tiled=True)
    gate_f = gate.astype(jnp.float32)
    up_f = up.astype(jnp.float32)
    sig = jax.nn.sigmoid(gate_f)
    act = gate_f * sig
    hidden = (act * up_f).astype(jnp.bfloat16)
    slabs = jnp.take(w_down, language, axis=0)
    received = lax.all_to_all(slabs, "dp", split_axis=0, concat_axis=2, tiled=True)
    weights = received[0]
    d_hidden = lax.dot_general(
        out_rows, weights, (((1,), (1,)), ((), ())), preferred_element_type=jnp.float32
    )
    d_up = (d_hidden * act).astype(jnp.bfloat16)
    d_gate = (d_hidden * up_f * sig * (1.0 + gate_f * (1.0 - sig))).astype(jnp.bfloat16)
    selector = (language[None, :] == jnp.arange(variants, dtype=jnp.int32)[:, None]).astype(
        jnp.float32
    )
    partial_term = lax.dot_general(
        hidden, out_rows, (((0,), (0,)), ((), ())), preferred_element_type=jnp.float32
    )
    pieces = lax.all_to_all(
        partial_term.reshape(ff_dev, groups, feat_dev),
        "dp",
        split_axis=1,
        concat_axis=1,
        tiled=True,
    )
    d_weight = jnp.einsum("lg,fgd->lfd", selector, pieces, precision=lax.Precision.HIGHEST)
    return (d_gate, d_up, d_weight)


def solution(mesh):
    return jax.shard_map(
        shards,
        mesh=mesh,
        in_specs=(
            P(("dp", "tensor"), None),
            P("dp", "tensor"),
            P("dp", "tensor"),
            P(None, "tensor", "dp"),
            P(),
        ),
        out_specs=(P("dp", "tensor"), P("dp", "tensor"), P(None, "tensor", "dp")),
        check_vma=False,
    )
```

profile of v0, /device:TPU:64, one launch (start us, length us, event | category | flops | bytes accessed | tf_op | source)
XLA Modules:
  0.0 566.6 jit_solution(13106661074899269644)
XLA Ops:
  7.2 0.0 copy-start
  7.2 0.8 compare_and_fusion
  8.0 0.7 compare_select_fusion
  8.6 0.0 copy-done
  8.7 4.0 gather_fusion
  12.7 6.9 %broadcast_select_fusion = bf16[16,896,256]{2,1,0:T(8,128)(2,1)} fusion(bf16[16,896,256]{2,1,0:T(8,128)(2,1)} %gather_fusion, pred[16]{0:T(512)(128)(4,1)S(1)} %compare_and_fusion), kind=kLoop, calls=%fused_computation.4 | loop fusion | flops 3670016 | bytes 14680080 | tf_op jit(solution)/shard_map/jit(_take)/select_n | solution.py:18
  19.6 0.0 copy-start.2
  19.6 0.0 copy-start.3
  19.6 8.2 %all-to-all-start = ((bf16[16,896,256]{2,1,0:T(8,128)(2,1)}), bf16[16,896,256]{2,1,0:T(8,128)(2,1)}, u32[]{:S(2)}, u32[]{:S(2)}) async-start(bf16[16,896,256]{2,1,0:T(8,128)(2,1)} %broadcast_select_fusion), calls=%async_computation | async-start | bytes 14680064 | tf_op jit(solution)/shard_map/all_to_all | solution.py:19
  27.7 0.0 all-gather.2.cloned.1.call-start
  27.8 0.7 all-gather.2.cloned.1.call-update
  28.5 0.0 copy-done.2
  28.5 0.5 copy.26
  29.0 0.0 copy-done.3
  29.0 0.5 copy.25
  29.6 121.4 %all-gather.2.cloned.1.call-done = bf16[512,4096]{1,0:T(8,128)(2,1)} async-done(((bf16[32,4096]{1,0:T(8,128)(2,1)}), bf16[512,4096]{1,0:T(8,128)(2,1)}) %all-gather.2.cloned.1.call-update) | async-done | bytes 4194320 | tf_op jit(solution)/shard_map/all_gather | solution.py:12
  150.9 9.5 %fusion.11 = f32[896,4096]{1,0:T(8,128)} fusion(bf16[512,4096]{1,0:T(8,128)(2,1)} %all-gather.2.cloned.1.call-done, bf16[512,896]{0,1:T(8,128)(2,1)S(1)} %copy.25, bf16[512,896]{0,1:T(8,128)(2,1)S(1)} %copy.26), kind=kOutput, calls=%fused_computation.20 | convolution fusion | flops 3761766400 | bytes 20709376 | tf_op jit(solution)/shard_map/dot_general | solution.py:29
  160.4 12.0 %copy.36 = f32[112,16,8,256]{3,2,0,1:T(8,128)} copy(f32[112,16,8,256]{3,2,1,0:T(8,128)} %bitcast.20) | data formatting | bytes 29360128 | tf_op jit(solution)/shard_map/reshape | solution.py:33
  172.4 44.2 %all-to-all-done = bf16[16,896,256]{2,1,0:T(8,128)(2,1)} async-done(((bf16[16,896,256]{2,1,0:T(8,128)(2,1)}), bf16[16,896,256]{2,1,0:T(8,128)(2,1)}, u32[]{:S(2)}, u32[]{:S(2)}) %all-to-all-start) | async-done | bytes 7340064 | tf_op jit(solution)/shard_map/all_to_all | solution.py:19
  216.6 5.2 all-to-all-start.1
  221.7 11.1 %copy.24 = bf16[1,896,16,256]{1,3,2,0:T(8,128)(2,1)} copy(bf16[1,896,16,256]{3,1,2,0:T(8,128)(2,1)} %bitcast.1) | data formatting | bytes 14680064 | tf_op jit(solution)/shard_map/all_to_all | solution.py:19
  232.9 9.8 %fusion.10 = (bf16[512,896]{0,1:T(8,128)(2,1)}, bf16[512,896]{0,1:T(8,128)(2,1)S(1)}) fusion(bf16[512,896]{0,1:T(8,128)(2,1)S(1)} %copy.26, bf16[512,896]{0,1:T(8,128)(2,1)S(1)} %copy.25, bf16[896,4096]{0,1:T(8,128)(2,1)} %bitcast.21, bf16[512,4096]{1,0:T(8,128)(2,1)} %all-gather.2.cloned.1.call-done), kind=kOutput, calls=%fused_computation.19 | convolution fusion | flops 3764977664 | bytes 15204352 | tf_op jit(solution)/shard_map/dot_general | solution.py:21
  242.7 0.0 copy-start.4
  242.7 2.2 copy.30
  244.9 1.3 copy.29
  246.2 292.8 %all-to-all-done.1 = f32[896,16,256]{2,0,1:T(8,128)} async-done(((f32[896,16,256]{2,0,1:T(8,128)}), f32[896,16,256]{2,0,1:T(8,128)}, u32[]{:S(2)}, u32[]{:S(2)}) %all-to-all-start.1) | async-done | bytes 14680096 | tf_op jit(solution)/shard_map/all_to_all | solution.py:32
  539.0 0.0 copy-done.4
  539.0 0.0 copy-start.1
  539.0 18.3 %fusion = f32[4,896,256]{2,0,1:T(4,128)S(1)} fusion(f32[896,16,256]{2,0,1:T(8,128)} %all-to-all-done.1, s32[16]{0:T(128)S(1)} %copy-done.4), kind=kOutput, calls=%fused_computation.2 | convolution fusion | flops 176160832 | bytes 18350144 | tf_op jit(solution)/shard_map/lg,fgd->lfd/dot_general | solution.py:39
  557.3 2.5 copy.31
  559.8 0.0 copy-done.1
  (1 shorter events, 0.0 us)
Async XLA Ops:
  7.2 1.5 copy-start
  19.6 8.9 %copy-start.2 = (bf16[512,896]{1,0:T(8,128)(2,1)S(1)}, bf16[512,896]{1,0:T(8,128)(2,1)}, u32[]{:S(2)}) copy-start(bf16[512,896]{1,0:T(8,128)(2,1)} %param.6) | copy-start | bytes 2752516
  19.6 9.4 %copy-start.3 = (bf16[512,896]{1,0:T(8,128)(2,1)S(1)}, bf16[512,896]{1,0:T(8,128)(2,1)}, u32[]{:S(2)}) copy-start(bf16[512,896]{1,0:T(8,128)(2,1)} %param.7) | copy-start | bytes 2752516
  19.6 197.0 %all-to-all-start = ((bf16[16,896,256]{2,1,0:T(8,128)(2,1)}), bf16[16,896,256]{2,1,0:T(8,128)(2,1)}, u32[]{:S(2)}, u32[]{:S(2)}) async-start(bf16[16,896,256]{2,1,0:T(8,128)(2,1)} %broadcast_select_fusion), calls=%async_computation | async-start | bytes 14680064 | tf_op jit(solution)/shard_map/all_to_all | solution.py:19
  27.7 123.2 %all-gather.2.cloned.1.call-start = ((), (), s32[]{:S(2)}) async-start(), calls=%async_computation.2 | async-start | bytes 4456448 | tf_op jit(solution)/shard_map/all_gather | solution.py:12
  216.6 322.4 %all-to-all-start.1 = ((f32[896,16,256]{2,0,1:T(8,128)}), f32[896,16,256]{2,0,1:T(8,128)}, u32[]{:S(2)}, u32[]{:S(2)}) async-start(f32[896,16,256]{2,0,1:T(8,128)} %bitcast.19), calls=%async_computation.1 | async-start | bytes 29360128 | tf_op jit(solution)/shard_map/all_to_all | solution.py:32
  242.7 296.3 %copy-start.4 = (s32[16]{0:T(128)S(1)}, s32[16]{0:T(128)}, u32[]{:S(2)}) copy-start(s32[16]{0:T(128)} %param.9) | copy-start | bytes 196
  539.0 20.8 %copy-start.1 = (bf16[4,896,256]{2,1,0:T(8,128)(2,1)S(1)}, bf16[4,896,256]{2,1,0:T(8,128)(2,1)}, u32[]{:S(2)}) copy-start(bf16[4,896,256]{2,1,0:T(8,128)(2,1)} %param.8) | copy-start | bytes 5505028
Sparse Core Ops, SparseCore 0:
  31.3 119.5 all-gather.1
where the time goes:
time: 567 us
  waiting for transfers between devices  459 us (81%)
  matrix products  37.6 us (7%)
  local copies, waits for them, and re-layouts  34.2 us (6%)
  between operations  14.1 us (2%)
  starting transfers between devices  13.4 us (2%)
  other arithmetic  8.33 us (1%)
    all_to_all x1, waiting for transfers between devices, shards(): lax.all_to_all(partial_term.reshape(ff_dev, groups, feat_dev), 'dp', spli...  293 us
    all_gather x1, waiting for transfers between devices, shards(): out_rows = lax.all_gather(cotangent, 'tensor', axis=0, tiled=True)  121 us
    all_to_all x1, waiting for transfers between devices, shards(): lax.all_to_all(slabs, 'dp', split_axis=0, concat_axis=2, tiled=True)  44.2 us
    dot_general x1, matrix products, shards(): jnp.einsum('lg,fgd->lfd', selector, pieces, precision=lax.Precision.HIGHEST)  18.3 us
    reshape x1, local copies, waits for them, and re-layouts, shards(): partial_term.reshape(ff_dev, groups, feat_dev)  12 us
  transfers between devices with their start and end apart: 3, of which 3 were waited for; matrix products, arithmetic and copies ran while one was open for 8% of the time, Pallas kernels for 0%

commit v1 on v0

--- a/solution.py
+++ b/solution.py
@@ -29,13 +29,14 @@
     partial_term = lax.dot_general(
         hidden, out_rows, (((0,), (0,)), ((), ())), preferred_element_type=jnp.float32
     )
-    pieces = lax.all_to_all(
-        partial_term.reshape(ff_dev, groups, feat_dev),
-        "dp",
-        split_axis=1,
-        concat_axis=1,
-        tiled=True,
+    mine_x = partial_term.reshape(ff_dev, groups, feat_dev)
+    carry_in = lax.all_to_all(
+        jnp.stack(jnp.split(mine_x, lax.psum(1, axis_name="dp"), 1)),
+        axis_name="dp",
+        split_axis=0,
+        concat_axis=0,
     )
+    pieces = jnp.concatenate(carry_in, 1)
     d_weight = jnp.einsum("lg,fgd->lfd", selector, pieces, precision=lax.Precision.HIGHEST)
     return (d_gate, d_up, d_weight)
 

time: 567 us -> 608 us (1.072)
  local copies, waits for them, and re-layouts: 34.2 us -> 110 us
  waiting for transfers between devices: 459 us -> 417 us
  starting transfers between devices: 13.4 us -> 20.7 us
    split x0 -> x1, local copies, waits for them, and re-layouts: none -> 44.2 us  [shards(): jnp.split(mine_x, lax.psum(1, axis_name='dp'), 1)]
    all_to_all x1, waiting for transfers between devices: 44.2 us -> 0.01 us  [shards(): lax.all_to_all(slabs, 'dp', split_axis=0, concat_axis=2, tiled=True)]
    unnamed x15 -> x49, local copies, waits for them, and re-layouts: 7.12 us -> 49.5 us
    reshape x1 -> x0, local copies, waits for them, and re-layouts: 12 us -> none  [shards(): partial_term.reshape(ff_dev, groups, feat_dev)]
    all_to_all x1, starting transfers between devices: 5.16 us -> 12.6 us  [shards(): lax.all_to_all(jnp.stack(jnp.split(mine_x, lax.psum(1, axis_name='dp'), 1...]
  transfers between devices with their start and end apart: 3 -> 3, of which waited for: 3 -> 2; matrix products, arithmetic and copies ran while one was open for 8% -> 22% of each run, Pallas kernels for 0% -> 0%
where the time goes in v1:
time: 608 us; the launch traced here: 607 us
  waiting for transfers between devices  417 us (69%)
  local copies, waits for them, and re-layouts  110 us (18%)
  matrix products  37.5 us (6%)
  starting transfers between devices  20.7 us (3%)
  between operations  14.2 us (2%)
  other arithmetic  7.66 us (1%)
    all_to_all x1, waiting for transfers between devices, shards(): lax.all_to_all(jnp.stack(jnp.split(mine_x, lax.psum(1, axis_name='dp'), 1...  294 us
    all_gather x1, waiting for transfers between devices, shards(): out_rows = lax.all_gather(cotangent, 'tensor', axis=0, tiled=True)  122 us
    unnamed x49, local copies, waits for them, and re-layouts  49.5 us
    split x1, local copies, waits for them, and re-layouts, shards(): jnp.split(mine_x, lax.psum(1, axis_name='dp'), 1)  44.2 us
    dot_general x1, matrix products, shards(): jnp.einsum('lg,fgd->lfd', selector, pieces, precision=lax.Precision.HIGHEST)  18.1 us
    all_to_all x1, starting transfers between devices, shards(): lax.all_to_all(jnp.stack(jnp.split(mine_x, lax.psum(1, axis_name='dp'), 1...  12.6 us
  transfers between devices with their start and end apart: 3, of which 2 were waited for; matrix products, arithmetic and copies ran while one was open for 22% of the time, Pallas kernels for 0%

profile of v1, /device:TPU:64, one launch (start us, length us, event | category | flops | bytes accessed | tf_op | source)
XLA Modules:
  0.0 606.6 jit_solution(5382738635096756557)
XLA Ops:
  7.2 0.7 all-gather.2.cloned.1.call-update
  8.7 4.0 gather_fusion
  12.7 7.0 %broadcast_select_fusion = bf16[16,896,256]{2,1,0:T(8,128)(2,1)} fusion(bf16[16,896,256]{2,1,0:T(8,128)(2,1)} %gather_fusion, pred[16]{0:T(512)(128)(4,1)S(1)} %compare_and_fusion), kind=kLoop, calls=%fused_computation.4 | loop fusion | flops 3670016 | bytes 14680080 | tf_op jit(solution)/shard_map/jit(_take)/select_n | solution.py:18
  19.7 8.0 %all-to-all-start = ((bf16[16,896,256]{2,1,0:T(8,128)(2,1)}), bf16[16,896,256]{2,1,0:T(8,128)(2,1)}, u32[]{:S(2)}, u32[]{:S(2)}) async-start(bf16[16,896,256]{2,1,0:T(8,128)(2,1)} %broadcast_select_fusion), calls=%async_computation | async-start | bytes 14680064 | tf_op jit(solution)/shard_map/all_to_all | solution.py:19
  28.9 122.2 %all-gather.2.cloned.1.call-done = bf16[512,4096]{1,0:T(8,128)(2,1)} async-done(((bf16[32,4096]{1,0:T(8,128)(2,1)}), bf16[512,4096]{1,0:T(8,128)(2,1)}) %all-gather.2.cloned.1.call-update) | async-done | bytes 4194320 | tf_op jit(solution)/shard_map/all_gather | solution.py:12
  151.0 9.6 %fusion.12 = f32[896,4096]{1,0:T(8,128)} fusion(bf16[512,4096]{1,0:T(8,128)(2,1)} %all-gather.2.cloned.1.call-done, bf16[512,896]{0,1:T(8,128)(2,1)S(1)} %copy.70, bf16[512,896]{0,1:T(8,128)(2,1)S(1)} %copy.71), kind=kOutput, calls=%fused_computation.20 | convolution fusion | flops 3761766400 | bytes 20709376 | tf_op jit(solution)/shard_map/dot_general | solution.py:29
  160.6 17.4 %copy.108 = f32[112,8,16,256]{3,2,1,0:T(8,128)} copy(f32[112,8,16,256]{3,1,2,0:T(8,128)} %bitcast.87) | data formatting | bytes 29360128
  178.0 44.2 %fusion.34 = (f32[896,1,256]{2,1,0:T(1,128)S(1)}, f32[896,1,256]{2,1,0:T(1,128)S(1)}, f32[896,1,256]{2,1,0:T(1,128)S(1)}, f32[896,1,256]{2,1,0:T(1,128)}, f32[89...) fusion(f32[896,16,256]{2,1,0:T(8,128)} %bitcast.86), kind=kLoop, calls=%fused_computation.60 | loop fusion | bytes 29360128 | tf_op jit(solution)/shard_map/split | solution.py:34
  222.3 2.3 fusion.29
  224.6 2.2 fusion.28
  226.8 2.2 fusion.27
  229.0 2.2 fusion.26
  231.2 2.2 fusion.25
  233.3 2.2 fusion.24
  235.5 2.3 fusion.23
  237.8 2.3 fusion.22
  240.0 1.0 fusion.21
  241.0 1.0 fusion.20
  242.0 1.0 fusion.19
  243.0 1.1 fusion.18
  244.1 1.0 fusion.17
  245.1 1.0 fusion.16
  246.1 1.0 fusion.15
  247.1 1.0 fusion.14
  248.1 12.6 %all-to-all-start.1 = ((f32[16,896,1,256]{3,1,2,0:T(8,128)}), f32[16,896,1,256]{3,1,2,0:T(8,128)}, u32[]{:S(2)}, u32[]{:S(2)}) async-start(f32[16,896,1,256]{3,1,2,0:T(8,128)} %fusion.14), calls=%async_computation.1 | async-start | bytes 29360128 | tf_op jit(solution)/shard_map/all_to_all | solution.py:33
  260.7 11.3 %copy.69 = bf16[1,896,16,256]{1,3,2,0:T(8,128)(2,1)} copy(bf16[1,896,16,256]{3,1,2,0:T(8,128)(2,1)} %bitcast.1) | data formatting | bytes 14680064 | tf_op jit(solution)/shard_map/all_to_all | solution.py:19
  272.0 9.8 %fusion.11 = (bf16[512,896]{0,1:T(8,128)(2,1)}, bf16[512,896]{0,1:T(8,128)(2,1)S(1)}) fusion(bf16[512,896]{0,1:T(8,128)(2,1)S(1)} %copy-done.10, bf16[512,896]{0,1:T(8,128)(2,1)S(1)} %copy-done.12, bf16[896,4096]{0,1:T(8,128)(2,1)} %bitcast.88, bf16[512,4096]{1,0:T(8,128)(2,1)} %all-gather.2.cloned.1.call-done), kind=kOutput, calls=%fused_computation.19 | convolution fusion | flops 3764977664 | bytes 15204352 | tf_op jit(solution)/shard_map/dot_general | solution.py:21
  281.8 2.3 copy.90
  284.1 1.3 copy.89
  285.4 293.7 %all-to-all-done.1 = f32[16,896,1,256]{3,1,2,0:T(8,128)} async-done(((f32[16,896,1,256]{3,1,2,0:T(8,128)}), f32[16,896,1,256]{3,1,2,0:T(8,128)}, u32[]{:S(2)}, u32[]{:S(2)}) %all-to-all-start.1) | async-done | bytes 14680096 | tf_op jit(solution)/shard_map/all_to_all | solution.py:33
  579.1 18.1 %fusion = f32[4,896,256]{2,0,1:T(4,128)S(1)} fusion(f32[16,896,1,256]{3,1,2,0:T(8,128)} %all-to-all-done.1, s32[16]{0:T(128)S(1)} %copy-done.13), kind=kOutput, calls=%fused_computation.1 | convolution fusion | flops 176160832 | bytes 18350144 | tf_op jit(solution)/shard_map/lg,fgd->lfd/dot_general | solution.py:40
  597.3 2.5 copy.91
  (35 shorter events, 1.9 us)
Async XLA Ops:
  7.2 1.5 copy-start
  7.2 5.5 copy-start.13
  7.2 143.8 %all-gather.2.cloned.1.call-start = ((), (), s32[]{:S(2)}) async-start(), calls=%async_computation.2 | async-start | bytes 4456448 | tf_op jit(solution)/shard_map/all_gather | solution.py:12
  12.7 15.0 %copy-start.7 = (bf16[512,896]{1,0:T(8,128)(2,1)S(1)}, bf16[512,896]{1,0:T(8,128)(2,1)}, u32[]{:S(2)}) copy-start(bf16[512,896]{1,0:T(8,128)(2,1)} %param.6) | copy-start | bytes 2752516
  12.7 15.6 %copy-start.8 = (bf16[512,896]{1,0:T(8,128)(2,1)S(1)}, bf16[512,896]{1,0:T(8,128)(2,1)}, u32[]{:S(2)}) copy-start(bf16[512,896]{1,0:T(8,128)(2,1)} %param.7) | copy-start | bytes 2752516
  19.7 228.4 %all-to-all-start = ((bf16[16,896,256]{2,1,0:T(8,128)(2,1)}), bf16[16,896,256]{2,1,0:T(8,128)(2,1)}, u32[]{:S(2)}, u32[]{:S(2)}) async-start(bf16[16,896,256]{2,1,0:T(8,128)(2,1)} %broadcast_select_fusion), calls=%async_computation | async-start | bytes 14680064 | tf_op jit(solution)/shard_map/all_to_all | solution.py:19
  28.3 149.7 %copy-start.9 = (bf16[512,896]{0,1:T(8,128)(2,1)}, bf16[512,896]{0,1:T(8,128)(2,1)S(1)}, u32[]{:S(2)}) copy-start(bf16[512,896]{0,1:T(8,128)(2,1)S(1)} %copy.71) | copy-start | bytes 2752516
  28.8 149.2 %copy-start.11 = (bf16[512,896]{0,1:T(8,128)(2,1)}, bf16[512,896]{0,1:T(8,128)(2,1)S(1)}, u32[]{:S(2)}) copy-start(bf16[512,896]{0,1:T(8,128)(2,1)S(1)} %copy.70) | copy-start | bytes 2752516
  222.2 17.8 %copy-start.6 = (f32[896,1,256]{2,1,0:T(1,128)S(1)}, f32[896,1,256]{2,1,0:T(1,128)}, u32[]{:S(2)}) copy-start(f32[896,1,256]{2,1,0:T(1,128)} %get-tuple-element.22) | copy-start | bytes 2752516
  222.2 18.8 %copy-start.5 = (f32[896,1,256]{2,1,0:T(1,128)S(1)}, f32[896,1,256]{2,1,0:T(1,128)}, u32[]{:S(2)}) copy-start(f32[896,1,256]{2,1,0:T(1,128)} %get-tuple-element.21) | copy-start | bytes 2752516
  222.3 19.7 %copy-start.4 = (f32[896,1,256]{2,1,0:T(1,128)S(1)}, f32[896,1,256]{2,1,0:T(1,128)}, u32[]{:S(2)}) copy-start(f32[896,1,256]{2,1,0:T(1,128)} %get-tuple-element.20) | copy-start | bytes 2752516
  222.3 20.7 %copy-start.3 = (f32[896,1,256]{2,1,0:T(1,128)S(1)}, f32[896,1,256]{2,1,0:T(1,128)}, u32[]{:S(2)}) copy-start(f32[896,1,256]{2,1,0:T(1,128)} %get-tuple-element.19) | copy-start | bytes 2752516
  222.3 21.8 %copy-start.2 = (f32[896,1,256]{2,1,0:T(1,128)S(1)}, f32[896,1,256]{2,1,0:T(1,128)}, u32[]{:S(2)}) copy-start(f32[896,1,256]{2,1,0:T(1,128)} %get-tuple-element.18) | copy-start | bytes 2752516
  248.1 331.0 %all-to-all-start.1 = ((f32[16,896,1,256]{3,1,2,0:T(8,128)}), f32[16,896,1,256]{3,1,2,0:T(8,128)}, u32[]{:S(2)}, u32[]{:S(2)}) async-start(f32[16,896,1,256]{3,1,2,0:T(8,128)} %fusion.14), calls=%async_computation.1 | async-start | bytes 29360128 | tf_op jit(solution)/shard_map/all_to_all | solution.py:33
  260.7 11.3 %copy-start.10 = (bf16[512,896]{0,1:T(8,128)(2,1)S(1)}, bf16[512,896]{0,1:T(8,128)(2,1)}, u32[]{:S(2)}) copy-start(bf16[512,896]{0,1:T(8,128)(2,1)} %copy-done.9) | copy-start | bytes 2752516
  260.7 11.3 %copy-start.12 = (bf16[512,896]{0,1:T(8,128)(2,1)S(1)}, bf16[512,896]{0,1:T(8,128)(2,1)}, u32[]{:S(2)}) copy-start(bf16[512,896]{0,1:T(8,128)(2,1)} %copy-done.11) | copy-start | bytes 2752516
  281.8 318.0 %copy-start.1 = (bf16[4,896,256]{2,1,0:T(8,128)(2,1)S(1)}, bf16[4,896,256]{2,1,0:T(8,128)(2,1)}, u32[]{:S(2)}) copy-start(bf16[4,896,256]{2,1,0:T(8,128)(2,1)} %param.8) | copy-start | bytes 5505028
Sparse Core Ops, SparseCore 0:
  10.8 140.2 all-gather.1
